TPU v7x, 256 devices: a whole 4x4x8 slice. The times are simulated.
256 devices in a mesh: graph: 8 (over z), index: 32 (over x, y, core).
Axes of the slice: x: 4, y: 4, z: 8, core: 2. Of those that a mesh axis runs over, the one named last changes fastest.
Arguments:
- features: bfloat16 [65536, 1024], P(('graph', 'index')), may hold values from -6 to 6
- q_weight: bfloat16 [1024, 1024], replicated, may hold values from -0.1875 to 0.1875
- q_bias: float32 [1024], replicated, may hold values from -3 to 3
- w_self: bfloat16 [1024, 1024], replicated, may hold values from -0.125 to 0.125
- w_neigh: bfloat16 [1024, 1024], replicated, may hold values from -0.125 to 0.125
- z_bias: float32 [1024], replicated, may hold values from -3 to 3
- centroids: bfloat16 [8192, 1024], P('index'), may hold values from -0.1875 to 0.1875
- requests: int32 [256, 32, 16], P(('graph', 'index')), may hold values from 0 to 255, as said below
- slots: int32 [65536, 50], P(('graph', 'index')), may hold values from 0 to 511
- importance: float32 [65536, 50], P(('graph', 'index')), may hold values from 0.1 to 10
- labels: int32 [65536, 1], P(('graph', 'index')), may hold values from 0 to 31; in each aligned block of 256 rows (0 to 255, 256 to 511, ...) at most 16 rows name the same one
Outputs:
- scores: bfloat16 [65536, 256], P(('graph', 'index'))
Inputs may be any that keep to these rules, and one draw needn't show every extreme that they name: `requests`: the 16 rows that a device asks of one device are distinct. `labels`: the rows of one device carry any one label at most 16 times.
All inputs are finite; a program needn't handle non-finite values.
Results may differ from a plain program's by a relative error of at most 0.0051.
Values may be sent and summed in bfloat16 or wider, within the bound.
No kernel may reach another device: no remote copies, remote signals or barrier semaphores. Data moves between devices by JAX's collectives and lax.ppermute only.
A program may use at most 64 MiB of HBM per device.

v0:
```python
import jax
import jax.numpy as jnp
from jax import lax
from jax.sharding import PartitionSpec as P


def place_rows(label_rows, peer_count, owner_slots):
    hits = (label_rows[:, None] == jnp.arange(peer_count, dtype=jnp.int32)[None, :]).astype(
        jnp.int32
    )
    ranks = jnp.sum(hits * (jnp.cumsum(hits, axis=0) - 1), axis=1)
    return label_rows * owner_slots + ranks


def one_hot(index, count):
    return (index[:, None] == jnp.arange(count, dtype=jnp.int32)[None, :]).astype(jnp.bfloat16)


def body(
    features,
    q_weight,
    q_bias,
    w_self,
    w_neigh,
    z_bias,
    centroids,
    requests,
    slots,
    importance,
    labels,
):
    row_count = features.shape[0]
    width = features.shape[1]
    peer_count = lax.axis_size("index")
    owner_slots = max(2 * row_count // peer_count, 2)
    fetch_slots = requests.shape[2]
    slot_count = peer_count * fetch_slots
    cent_count = centroids.shape[0]
    me = lax.axis_index("index")
    own_rows = jnp.where(
        jnp.arange(peer_count, dtype=jnp.int32)[:, None, None] == me,
        requests.astype(jnp.float32),
        0.0,
    )
    all_requests = lax.psum(own_rows, "index")
    wanted = lax.dynamic_index_in_dim(all_requests, me, axis=1, keepdims=False).astype(jnp.int32)
    messages = jax.nn.relu(
        jnp.dot(features, q_weight, preferred_element_type=jnp.float32) + q_bias
    ).astype(jnp.bfloat16)
    weights_norm = importance / jnp.sum(importance, axis=1, keepdims=True)
    slot_ids = jnp.arange(slot_count, dtype=jnp.int32)
    mixing = jnp.sum(
        jnp.where(slots[:, :, None] == slot_ids[None, None, :], weights_norm[:, :, None], 0.0),
        axis=1,
    ).astype(jnp.bfloat16)
    outgoing_msgs = jnp.dot(
        one_hot(wanted.reshape(-1), row_count),
        lax.optimization_barrier(messages),
        preferred_element_type=jnp.float32,
    ).astype(jnp.bfloat16)
    fetched = lax.all_to_all(
        outgoing_msgs.reshape(peer_count, fetch_slots, width),
        "index",
        split_axis=0,
        concat_axis=0,
        tiled=True,
    ).reshape(slot_count, width)
    pooled = jnp.dot(mixing, fetched, preferred_element_type=jnp.float32).astype(jnp.bfloat16)
    hidden = jax.nn.relu(
        jnp.dot(features, w_self, preferred_element_type=jnp.float32)
        + jnp.dot(pooled, w_neigh, preferred_element_type=jnp.float32)
        + z_bias
    )
    normed = (hidden * lax.rsqrt(jnp.mean(hidden * hidden, axis=1, keepdims=True) + 1e-06)).astype(
        jnp.bfloat16
    )
    positions = place_rows(labels[:, 0], peer_count, owner_slots)
    pick = one_hot(positions, peer_count * owner_slots)
    outgoing = lax.dot_general(
        pick, normed, (((0,), (0,)), ((), ())), preferred_element_type=jnp.float32
    ).astype(jnp.bfloat16)
    outgoing = outgoing.reshape(peer_count, owner_slots, width)
    arrived = lax.all_to_all(outgoing, "index", split_axis=0, concat_axis=0, tiled=True)
    flat_rows = arrived.reshape(-1, width)
    raw_scores = lax.dot_general(
        flat_rows, centroids, (((1,), (1,)), ((), ())), preferred_element_type=jnp.float32
    ).astype(jnp.bfloat16)
    returned = lax.all_to_all(
        raw_scores.reshape(peer_count, arrived.shape[1], cent_count),
        "index",
        split_axis=0,
        concat_axis=0,
        tiled=True,
    )
    return jnp.dot(
        pick,
        returned.reshape(peer_count * owner_slots, cent_count),
        preferred_element_type=jnp.float32,
    ).astype(jnp.bfloat16)


def solution(mesh):
    return jax.shard_map(
        body,
        mesh=mesh,
        in_specs=(
            P(("graph", "index"), None),
            P(),
            P(),
            P(),
            P(),
            P(),
            P("index", None),
            P(("graph", "index"), None, None),
            P(("graph", "index"), None),
            P(("graph", "index"), None),
            P(("graph", "index"), None),
        ),
        out_specs=P(("graph", "index"), None),
        check_vma=False,
    )
```

profile of v0, /device:TPU:1, one launch (start us, length us, event | category | flops | bytes accessed | tf_op | source)
XLA Modules:
  0.0 201.9 jit_solution(17790053467064373194)
XLA Ops:
  6.5 0.0 copy-start
  6.5 0.0 all-reduce.2.cloned.1.call-start
  6.5 0.8 convert_bitcast_fusion
  7.4 0.1 copy.20
  7.5 0.9 broadcast_select_fusion
  8.4 0.0 copy-start.6
  8.4 0.0 all-reduce.2.cloned.1.call-update
  8.4 0.7 fusion.12
  9.1 0.6 reduce-window.6
  9.7 0.2 slice_reduce_fusion
  9.9 0.0 copy-start.4
  9.9 2.6 %fusion.13 = f32[256,1024]{1,0:T(8,128)S(1)} fusion(bf16[256,1024]{1,0:T(8,128)(2,1)} %param.11, bf16[1024,1024]{1,0:T(8,128)(2,1)} %param.14), kind=kOutput, calls=%fused_computation.37 | convolution fusion | flops 536870912 | bytes 3670016 | tf_op jit(solution)/shard_map/dot_general | solution.py:70
  12.6 0.0 copy-done.6
  12.6 0.0 copy-done.4
  12.6 0.0 copy-start.3
  12.6 2.6 %fusion.3 = bf16[256,1024]{1,0:T(8,128)(2,1)} fusion(bf16[256,1024]{1,0:T(8,128)(2,1)} %param.11, bf16[1024,1024]{1,0:T(8,128)(2,1)S(1)} %copy-done.4, f32[1024]{0:T(1024)S(1)} %copy-done.6), kind=kOutput, calls=%fused_computation.9 | convolution fusion | flops 537657344 | bytes 3149824 | tf_op jit(solution)/shard_map/dot_general | solution.py:48
  15.1 0.0 copy-start.1
  15.1 0.0 copy-start.2
  15.1 0.0 copy-done.3
  15.1 0.1 fusion.11
  15.2 113.5 %all-reduce.2.cloned.1.call-done = f32[32,32,16]{2,0,1:T(8,128)} async-done(((f32[32,32,16]{2,0,1:T(8,128)}), f32[32,32,16]{2,0,1:T(8,128)}) %all-reduce.2.cloned.1.call-update) | async-done | bytes 65552 | tf_op jit(solution)/shard_map/psum | solution.py:45
  128.7 0.7 dynamic-slice_convert_fusion
  129.4 0.1 convert_element_type.48
  129.5 0.0 copy-start.7
  129.5 2.6 %convolution_convert_fusion.1 = bf16[512,1024]{1,0:T(8,128)(2,1)} fusion(bf16[256,1024]{1,0:T(8,128)(2,1)} %fusion.3, s32[512]{0:T(512)S(1)} %convert_element_type.48), kind=kOutput, calls=%fused_computation.3 | convolution fusion | flops 269090816 | bytes 1574912 | tf_op jit(solution)/shard_map/dot_general | solution.py:56
  132.1 6.1 %all-to-all-start = ((bf16[32,16,1024]{2,1,0:T(8,128)(2,1)}), bf16[32,16,1024]{2,1,0:T(8,128)(2,1)}, u32[]{:S(2)}, u32[]{:S(2)}) async-start(bf16[32,16,1024]{2,1,0:T(8,128)(2,1)} %bitcast.6), calls=%async_computation | async-start | bytes 2097152 | tf_op jit(solution)/shard_map/all_to_all | solution.py:61
  138.2 0.0 copy-done.1
  138.3 0.0 copy-done.2
  138.3 4.3 %select_reduce_fusion = bf16[256,512]{1,0:T(8,128)(2,1)S(1)} fusion(f32[256,50]{0,1:T(8,128)S(1)} %broadcast_divide_fusion, s32[256,50]{0,1:T(8,128)S(1)} %copy-done.2), kind=kLoop, calls=%fused_computation | loop fusion | flops 19529728 | bytes 364544 | tf_op jit(solution)/shard_map/reduce_sum | solution.py:52
  142.6 12.5 %all-to-all-done = bf16[32,16,1024]{2,1,0:T(8,128)(2,1)} async-done(((bf16[32,16,1024]{2,1,0:T(8,128)(2,1)}), bf16[32,16,1024]{2,1,0:T(8,128)(2,1)}, u32[]{:S(2)}, u32[]{:S(2)}) %all-to-all-start) | async-done | bytes 1048608 | tf_op jit(solution)/shard_map/all_to_all | solution.py:61
  155.1 0.0 copy-done
  155.1 0.0 copy-done.7
  155.2 3.3 %multiply_reduce_fusion = (f32[256]{0:T(256)S(1)}, f32[256,1024]{1,0:T(8,128)}) fusion(f32[1024]{0:T(1024)S(1)} %copy-done.7, f32[256,1024]{1,0:T(8,128)S(1)} %fusion.13, bf16[1024,1024]{1,0:T(8,128)(2,1)S(1)} %copy-done, bf16[512,1024]{1,0:T(8,128)(2,1)} %bitcast.7, bf16[256,512]{1,0:T(8,128)(2,1)S(1)} %select_reduce_fusion), kind=kOutput, calls=%fused_computation.14 | convolution fusion | flops 806878976 | bytes 5510144 | tf_op jit(solution)/shard_map/dot_general | solution.py:71
  158.4 0.0 copy-start.5
  158.4 1.8 convolution_convert_fusion
  160.3 20.6 %all_to_all.15 = bf16[32,16,1024]{2,1,0:T(8,128)(2,1)S(1)} all-to-all(bf16[32,16,1024]{2,1,0:T(8,128)(2,1)S(1)} %bitcast.40), channel_id=1, replica_groups=mesh['graph'=8,'index'=32] {'index'}, dimensions={0} | all-to-all | bytes 2097152 | tf_op jit(solution)/shard_map/all_to_all | solution.py:83
  180.9 0.0 copy-done.5
  180.9 0.5 convolution_convert_fusion.3
  181.4 12.7 %all_to_all.16 = bf16[32,16,256]{2,1,0:T(8,128)(2,1)S(1)} all-to-all(bf16[32,16,256]{2,1,0:T(8,128)(2,1)S(1)} %bitcast.43), channel_id=1, replica_groups=mesh['graph'=8,'index'=32] {'index'}, dimensions={0} | all-to-all | bytes 524288 | tf_op jit(solution)/shard_map/all_to_all | solution.py:88
  194.1 0.9 convolution_convert_fusion.4
  (7 shorter events, 0.1 us)
Async XLA Ops:
  6.5 148.6 %copy-start = (bf16[1024,1024]{1,0:T(8,128)(2,1)S(1)}, bf16[1024,1024]{1,0:T(8,128)(2,1)}, u32[]{:S(2)}) copy-start(bf16[1024,1024]{1,0:T(8,128)(2,1)} %param.15) | copy-start | bytes 6291460
  6.5 122.2 %all-reduce.2.cloned.1.call-start = ((), (), s32[]{:S(2)}) async-start(), calls=%async_computation.3 | async-start | bytes 1048576 | tf_op jit(solution)/shard_map/psum | solution.py:45
  8.4 4.1 %copy-start.6 = (f32[1024]{0:T(1024)S(1)}, f32[1024]{0:T(1024)}, u32[]{:S(2)}) copy-start(f32[1024]{0:T(1024)} %param.13) | copy-start | bytes 12292
  9.9 2.6 %copy-start.4 = (bf16[1024,1024]{1,0:T(8,128)(2,1)S(1)}, bf16[1024,1024]{1,0:T(8,128)(2,1)}, u32[]{:S(2)}) copy-start(bf16[1024,1024]{1,0:T(8,128)(2,1)} %param.12) | copy-start | bytes 6291460
  12.6 2.6 %copy-start.3 = (s32[256,1]{0,1:T(1,128)S(1)}, s32[256,1]{0,1:T(1,128)}, u32[]{:S(2)}) copy-start(s32[256,1]{0,1:T(1,128)} %param.21) | copy-start | bytes 3076
  15.1 123.1 %copy-start.1 = (f32[256,50]{0,1:T(8,128)S(1)}, f32[256,50]{0,1:T(8,128)}, u32[]{:S(2)}) copy-start(f32[256,50]{0,1:T(8,128)} %param.20) | copy-start | bytes 153604
  15.1 123.1 %copy-start.2 = (s32[256,50]{0,1:T(8,128)S(1)}, s32[256,50]{0,1:T(8,128)}, u32[]{:S(2)}) copy-start(s32[256,50]{0,1:T(8,128)} %param.19) | copy-start | bytes 153604
  129.5 25.6 %copy-start.7 = (f32[1024]{0:T(1024)S(1)}, f32[1024]{0:T(1024)}, u32[]{:S(2)}) copy-start(f32[1024]{0:T(1024)} %param.16) | copy-start | bytes 12292
  132.1 23.0 %all-to-all-start = ((bf16[32,16,1024]{2,1,0:T(8,128)(2,1)}), bf16[32,16,1024]{2,1,0:T(8,128)(2,1)}, u32[]{:S(2)}, u32[]{:S(2)}) async-start(bf16[32,16,1024]{2,1,0:T(8,128)(2,1)} %bitcast.6), calls=%async_computation | async-start | bytes 2097152 | tf_op jit(solution)/shard_map/all_to_all | solution.py:61
  158.4 22.5 %copy-start.5 = (bf16[256,1024]{1,0:T(8,128)(2,1)S(1)}, bf16[256,1024]{1,0:T(8,128)(2,1)}, u32[]{:S(2)}) copy-start(bf16[256,1024]{1,0:T(8,128)(2,1)} %param.17) | copy-start | bytes 1572868
Sparse Core Ops, SparseCore 0:
  10.5 118.1 all-reduce.1
where the time goes:
time: 202 us
  waiting for transfers between devices  126 us (62%)
  blocking collectives  33.3 us (16%)
  matrix products  14.3 us (7%)
  between operations  13.5 us (7%)
  other arithmetic  8.31 us (4%)
  starting transfers between devices  6.08 us (3%)
    psum x1, waiting for transfers between devices, body(): all_requests = lax.psum(own_rows, 'index')  113 us
    all_to_all x1, blocking collectives, body(): lax.all_to_all(outgoing, 'index', split_axis=0, concat_axis=0, tiled=True)  20.6 us
    all_to_all x1, blocking collectives, body(): lax.all_to_all(raw_scores.reshape(peer_count, arrived.shape[1], cent_coun...  12.7 us
    all_to_all x1, waiting for transfers between devices, body(): lax.all_to_all(outgoing_msgs.reshape(peer_count, fetch_slots, width), 'in...  12.5 us
    all_to_all x1, starting transfers between devices, body(): lax.all_to_all(outgoing_msgs.reshape(peer_count, fetch_slots, width), 'in...  6.08 us
    reduce_sum x1, other arithmetic, body(): jnp.sum(jnp.where(slots[:, :, None] == slot_ids[None, None, :], weights_n...  4.35 us
  transfers between devices with their start and end apart: 2, of which 2 were waited for; matrix products, arithmetic and copies ran while one was open for 6% of the time, Pallas kernels for 0%

commit v1 on v0

--- a/solution.py
+++ b/solution.py
@@ -2,6 +2,11 @@
 import jax.numpy as jnp
 from jax import lax
 from jax.sharding import PartitionSpec as P
+
+
+def _load_shapes(vec):
+    front = jnp.sum(lax.all_gather(vec, axis_name="index"), axis=0)
+    return front
 
 
 def place_rows(label_rows, peer_count, owner_slots):
@@ -42,7 +47,7 @@
         requests.astype(jnp.float32),
         0.0,
     )
-    all_requests = lax.psum(own_rows, "index")
+    all_requests = _load_shapes(own_rows)
     wanted = lax.dynamic_index_in_dim(all_requests, me, axis=1, keepdims=False).astype(jnp.int32)
     messages = jax.nn.relu(
         jnp.dot(features, q_weight, preferred_element_type=jnp.float32) + q_bias

time: 202 us -> 149 us (0.74)
  waiting for transfers between devices: 126 us -> 69.5 us
  other arithmetic: 8.31 us -> 11.6 us
    psum x1 -> x0, waiting for transfers between devices: 113 us -> none  [body(): all_requests = lax.psum(own_rows, 'index')]
    all_gather x0 -> x1, waiting for transfers between devices: none -> 57 us  [_load_shapes(): front = jnp.sum(lax.all_gather(vec, axis_name='index'), axis=0)]
    reduce_sum x0 -> x1, other arithmetic: none -> 4.04 us  [_load_shapes(): front = jnp.sum(lax.all_gather(vec, axis_name='index'), axis=0)]
  transfers between devices with their start and end apart: 2 -> 2, of which waited for: 2 -> 2; matrix products, arithmetic and copies ran while one was open for 6% -> 7% of each run, Pallas kernels for 0% -> 0%
where the time goes in v1:
time: 149 us
  waiting for transfers between devices  69.5 us (47%)
  blocking collectives  33.3 us (22%)
  matrix products  14.8 us (10%)
  between operations  13.5 us (9%)
  other arithmetic  11.6 us (8%)
  starting transfers between devices  5.54 us (4%)
    all_gather x1, waiting for transfers between devices, _load_shapes(): front = jnp.sum(lax.all_gather(vec, axis_name='index'), axis=0)  57 us
    all_to_all x1, blocking collectives, body(): lax.all_to_all(outgoing, 'index', split_axis=0, concat_axis=0, tiled=True)  20.6 us
    all_to_all x1, blocking collectives, body(): lax.all_to_all(raw_scores.reshape(peer_count, arrived.shape[1], cent_coun...  12.7 us
    all_to_all x1, waiting for transfers between devices, body(): lax.all_to_all(outgoing_msgs.reshape(peer_count, fetch_slots, width), 'in...  12.5 us
    all_to_all x1, starting transfers between devices, body(): lax.all_to_all(outgoing_msgs.reshape(peer_count, fetch_slots, width), 'in...  5.54 us
    reduce_sum x1, other arithmetic, body(): jnp.sum(jnp.where(slots[:, :, None] == slot_ids[None, None, :], weights_n...  4.35 us
    reduce_sum x1, other arithmetic, _load_shapes(): front = jnp.sum(lax.all_gather(vec, axis_name='index'), axis=0)  4.04 us
    dot_general x1, matrix products, body(): jnp.dot(pooled, w_neigh, preferred_element_type=jnp.float32)  3.27 us
  transfers between devices with their start and end apart: 2, of which 2 were waited for; matrix products, arithmetic and copies ran while one was open for 7% of the time, Pallas kernels for 0%

profile of v1, /device:TPU:1, one launch (start us, length us, event | category | flops | bytes accessed | tf_op | source)
XLA Modules:
  0.0 148.6 jit_solution(885160135929034312)
XLA Ops:
  6.5 0.0 copy-start
  6.5 0.0 all-gather.2.cloned.1.call-start
  6.5 0.8 convert_bitcast_fusion
  7.4 0.8 broadcast_select_fusion
  8.2 0.0 copy-start.3
  8.2 0.0 all-gather.2.cloned.1.call-update
  8.3 3.2 %fusion.3 = bf16[256,1024]{1,0:T(8,128)(2,1)} fusion(bf16[256,1024]{1,0:T(8,128)(2,1)} %param.11, bf16[1024,1024]{1,0:T(8,128)(2,1)} %param.12, f32[1024]{0:T(1024)} %param.13), kind=kOutput, calls=%fused_computation.9 | convolution fusion | flops 537657344 | bytes 3149824 | tf_op jit(solution)/shard_map/dot_general | solution.py:53
  11.5 0.0 copy-done.3
  11.5 0.6 reduce-window.6
  12.1 0.2 slice_reduce_fusion
  12.3 0.1 fusion.11
  12.4 2.5 %fusion.13 = f32[256,1024]{1,0:T(8,128)S(1)} fusion(bf16[256,1024]{1,0:T(8,128)(2,1)} %param.11, bf16[1024,1024]{1,0:T(8,128)(2,1)} %param.14), kind=kOutput, calls=%fused_computation.37 | convolution fusion | flops 536870912 | bytes 3670016 | tf_op jit(solution)/shard_map/dot_general | solution.py:75
  14.9 57.0 %all-gather.2.cloned.1.call-done = f32[32,32,32,16]{2,3,1,0:T(8,128)} async-done(((f32[1,32,32,16]{2,3,1,0:T(8,128)}), f32[32,32,32,16]{2,3,1,0:T(8,128)}) %all-gather.2.cloned.1.call-update) | async-done | bytes 2097168 | tf_op jit(solution)/shard_map/all_gather | solution.py:8
  71.9 4.0 %reduce_sum.51 = f32[32,32,16]{1,2,0:T(8,128)S(1)} reduce(f32[32,32,32,16]{2,3,1,0:T(8,128)} %all-gather.2.cloned.1.call-done, f32[]{:T(128)} %constant.25.clone.1), dimensions={0}, to_apply=%region_5.6 | reduce | flops 507904 | bytes 2162692 | tf_op jit(solution)/shard_map/reduce_sum | solution.py:8
  76.0 0.0 copy-start.1
  76.0 0.0 copy-start.2
  76.0 0.7 convert_reduce_fusion
  76.7 0.1 convert_element_type.48
  76.8 0.0 copy-start.5
  76.8 2.6 %convolution_convert_fusion.1 = bf16[512,1024]{1,0:T(8,128)(2,1)} fusion(bf16[256,1024]{1,0:T(8,128)(2,1)} %fusion.3, s32[512]{0:T(512)S(1)} %convert_element_type.48), kind=kOutput, calls=%fused_computation.3 | convolution fusion | flops 269090816 | bytes 1574912 | tf_op jit(solution)/shard_map/dot_general | solution.py:61
  79.4 5.5 %all-to-all-start = ((bf16[32,16,1024]{2,1,0:T(8,128)(2,1)}), bf16[32,16,1024]{2,1,0:T(8,128)(2,1)}, u32[]{:S(2)}, u32[]{:S(2)}) async-start(bf16[32,16,1024]{2,1,0:T(8,128)(2,1)} %bitcast.6), calls=%async_computation | async-start | bytes 2097152 | tf_op jit(solution)/shard_map/all_to_all | solution.py:66
  84.9 0.0 copy-done.1
  85.0 0.0 copy-done.2
  85.0 4.3 %select_reduce_fusion = bf16[256,512]{1,0:T(8,128)(2,1)S(1)} fusion(f32[256,50]{0,1:T(8,128)S(1)} %broadcast_divide_fusion, s32[256,50]{0,1:T(8,128)S(1)} %copy-done.2), kind=kLoop, calls=%fused_computation | loop fusion | flops 19529728 | bytes 364544 | tf_op jit(solution)/shard_map/reduce_sum | solution.py:57
  89.4 12.5 %all-to-all-done = bf16[32,16,1024]{2,1,0:T(8,128)(2,1)} async-done(((bf16[32,16,1024]{2,1,0:T(8,128)(2,1)}), bf16[32,16,1024]{2,1,0:T(8,128)(2,1)}, u32[]{:S(2)}, u32[]{:S(2)}) %all-to-all-start) | async-done | bytes 1048608 | tf_op jit(solution)/shard_map/all_to_all | solution.py:66
  101.9 0.0 copy-done
  101.9 0.0 copy-done.5
  101.9 3.3 %multiply_reduce_fusion = (f32[256]{0:T(256)S(1)}, f32[256,1024]{1,0:T(8,128)}) fusion(f32[1024]{0:T(1024)S(1)} %copy-done.5, f32[256,1024]{1,0:T(8,128)S(1)} %fusion.13, bf16[1024,1024]{1,0:T(8,128)(2,1)S(1)} %copy-done, bf16[512,1024]{1,0:T(8,128)(2,1)} %bitcast.7, bf16[256,512]{1,0:T(8,128)(2,1)S(1)} %select_reduce_fusion), kind=kOutput, calls=%fused_computation.14 | convolution fusion | flops 806878976 | bytes 5510144 | tf_op jit(solution)/shard_map/dot_general | solution.py:76
  105.2 0.0 copy-start.4
  105.2 1.8 %convolution_convert_fusion = bf16[512,1024]{1,0:T(8,128)(2,1)S(1)} fusion(f32[256,1024]{1,0:T(8,128)} %get-tuple-element.6, f32[256]{0:T(256)S(1)} %add_rsqrt_fusion, s32[256]{0:T(256)S(1)} %bitcast.44), kind=kOutput, calls=%fused_computation.2 | convolution fusion | flops 269615104 | bytes 2099200 | tf_op jit(solution)/shard_map/dot_general | solution.py:84
  107.0 20.6 %all_to_all.15 = bf16[32,16,1024]{2,1,0:T(8,128)(2,1)S(1)} all-to-all(bf16[32,16,1024]{2,1,0:T(8,128)(2,1)S(1)} %bitcast.38), channel_id=1, replica_groups=mesh['graph'=8,'index'=32] {'index'}, dimensions={0} | all-to-all | bytes 2097152 | tf_op jit(solution)/shard_map/all_to_all | solution.py:88
  127.7 0.0 copy-done.4
  127.7 0.5 convolution_convert_fusion.3
  128.1 12.7 %all_to_all.16 = bf16[32,16,256]{2,1,0:T(8,128)(2,1)S(1)} all-to-all(bf16[32,16,256]{2,1,0:T(8,128)(2,1)S(1)} %bitcast.41), channel_id=1, replica_groups=mesh['graph'=8,'index'=32] {'index'}, dimensions={0} | all-to-all | bytes 524288 | tf_op jit(solution)/shard_map/all_to_all | solution.py:93
  140.8 0.9 convolution_convert_fusion.4
  (8 shorter events, 0.1 us)
Async XLA Ops:
  6.5 95.3 %copy-start = (bf16[1024,1024]{1,0:T(8,128)(2,1)S(1)}, bf16[1024,1024]{1,0:T(8,128)(2,1)}, u32[]{:S(2)}) copy-start(bf16[1024,1024]{1,0:T(8,128)(2,1)} %param.15) | copy-start | bytes 6291460
  6.5 65.4 %all-gather.2.cloned.1.call-start = ((), (), s32[]{:S(2)}) async-start(), calls=%async_computation.3 | async-start | bytes 8650752 | tf_op jit(solution)/shard_map/all_gather | solution.py:8
  8.2 3.3 %copy-start.3 = (s32[256,1]{0,1:T(1,128)S(1)}, s32[256,1]{0,1:T(1,128)}, u32[]{:S(2)}) copy-start(s32[256,1]{0,1:T(1,128)} %param.21) | copy-start | bytes 3076
  76.0 9.0 %copy-start.1 = (f32[256,50]{0,1:T(8,128)S(1)}, f32[256,50]{0,1:T(8,128)}, u32[]{:S(2)}) copy-start(f32[256,50]{0,1:T(8,128)} %param.20) | copy-start | bytes 153604
  76.0 9.0 %copy-start.2 = (s32[256,50]{0,1:T(8,128)S(1)}, s32[256,50]{0,1:T(8,128)}, u32[]{:S(2)}) copy-start(s32[256,50]{0,1:T(8,128)} %param.19) | copy-start | bytes 153604
  76.8 25.1 %copy-start.5 = (f32[1024]{0:T(1024)S(1)}, f32[1024]{0:T(1024)}, u32[]{:S(2)}) copy-start(f32[1024]{0:T(1024)} %param.16) | copy-start | bytes 12292
  79.4 22.5 %all-to-all-start = ((bf16[32,16,1024]{2,1,0:T(8,128)(2,1)}), bf16[32,16,1024]{2,1,0:T(8,128)(2,1)}, u32[]{:S(2)}, u32[]{:S(2)}) async-start(bf16[32,16,1024]{2,1,0:T(8,128)(2,1)} %bitcast.6), calls=%async_computation | async-start | bytes 2097152 | tf_op jit(solution)/shard_map/all_to_all | solution.py:66
  105.2 22.5 %copy-start.4 = (bf16[256,1024]{1,0:T(8,128)(2,1)S(1)}, bf16[256,1024]{1,0:T(8,128)(2,1)}, u32[]{:S(2)}) copy-start(bf16[256,1024]{1,0:T(8,128)(2,1)} %param.17) | copy-start | bytes 1572868
Sparse Core Ops, SparseCore 0:
  9.9 61.9 all-gather.1
